TPU v7x, 256 devices: a whole 4x4x8 slice. The times are simulated.
256 devices in a mesh: fsdp: 32 (over y, x, z_hi), tp: 8 (over z_lo, core).
Axes of the slice: x: 4, y: 4, z: 8 (z_hi: 2, z_lo: 4; z = z_hi * 4 + z_lo), core: 2. Of those that a mesh axis runs over, the one named last changes fastest.
Arguments:
- tokens: bfloat16 [16384, 4096], P(('fsdp', 'tp')), may hold values from -6 to 6
- in_weight: bfloat16 [4096, 3, 4096], P('fsdp', None, 'tp'), may hold values from -0.09375 to 0.09375
- out_weight: bfloat16 [4096, 4096], P('fsdp', 'tp'), may hold values from -0.09375 to 0.09375
- short_taps: float32 [3, 3, 4096], P(None, None, 'tp'), may hold values from -3 to 3
- filter_taps: float32 [128, 4096], P(None, 'tp'), may hold values from -1.2 to 1.2
- decay_rate: float32 [4096], P('tp'), may hold values from 0.00390625 to 0.09375
- doc_lengths: int32 [64], replicated, may hold values from 1 to 2048, 16384 in all
Outputs:
- mixed_out: bfloat16 [16384, 4096], P(('fsdp', 'tp'))
Inputs may be any that keep to these rules, and one draw needn't show every extreme that they name: `doc_lengths`: the documents of the window in order; they sum to 16384.
All inputs are finite; a program needn't handle non-finite values.
Results may differ from a plain program's by a relative error of at most 0.014.
Values may be sent and summed in bfloat16 or wider, within the bound.
No kernel may reach another device: no remote copies, remote signals or barrier semaphores. Data moves between devices by JAX's collectives and lax.ppermute only.
A program may use at most 64 MiB of HBM per device.

v0:
```python
import jax
import jax.numpy as jnp
from jax import lax
from jax.sharding import Mesh
from jax.sharding import PartitionSpec as P

COL = ("zh", "zl", "c")


def doc_position(points, lengths):
    starts = jnp.cumsum(lengths) - lengths
    begins = jnp.max(jnp.where(starts[None, :] <= points[:, None], starts[None, :], 0), axis=1)
    return points - begins


def short_filter(extended, short_taps, positions, out_count):
    running = jnp.zeros((out_count,) + extended.shape[1:], jnp.float32)
    for tap_index in range(3):
        window = extended[2 - tap_index : 2 - tap_index + out_count].astype(jnp.float32)
        inside = (positions >= tap_index)[:, None, None]
        running = running + jnp.where(
            inside, short_taps[tap_index][None] * window, jnp.float32(0.0)
        )
    return running


def long_filter(extended, shaped, positions, out_count, tap_count):

    def tap_group(group_index, running):
        for inner in range(16):
            tap_index = group_index * 16 + inner
            window = lax.dynamic_slice_in_dim(extended, tap_count - tap_index, out_count, 0)
            weight_row = lax.dynamic_slice_in_dim(shaped, tap_index, 1, 0)
            inside = (positions >= tap_index)[:, None]
            running = running + jnp.where(
                inside, weight_row * window.astype(jnp.float32), jnp.float32(0.0)
            )
        return running

    zero_sum = jnp.zeros((out_count, shaped.shape[1]), jnp.float32)
    return lax.fori_loop(0, tap_count // 16, tap_group, zero_sum)


def swap_half(piece, zh, axis):
    width = piece.shape[axis] // 2
    lo = lax.slice_in_dim(piece, 0, width, axis=axis)
    hi = lax.slice_in_dim(piece, width, 2 * width, axis=axis)
    keep = jnp.where(zh == 0, lo, hi)
    give = jnp.where(zh == 0, hi, lo)
    got = lax.ppermute(give, "zh", [(0, 1), (1, 0)])
    first = jnp.where(zh == 0, keep, got)
    second = jnp.where(zh == 0, got, keep)
    return jnp.concatenate([first, second], 0)


def body(tokens, in_weight, out_weight, short_taps, filter_taps, decay_rate, doc_lengths):
    zh = lax.axis_index("zh")
    col_size = lax.axis_size("zh") * lax.axis_size("zl") * lax.axis_size("c")
    own_rows = tokens.shape[0]
    col_rows = own_rows * col_size
    half = in_weight.shape[2] // 2
    tap_count = filter_taps.shape[0]
    widened = tokens.astype(jnp.float32)
    normed = (
        widened * lax.rsqrt(jnp.mean(widened * widened, axis=1, keepdims=True) + 1e-06)
    ).astype(jnp.bfloat16)
    gathered = lax.all_gather(normed, COL, axis=0, tiled=True)
    in_piece = swap_half(in_weight, zh, 2)
    in_full = lax.all_gather(in_piece, "p", axis=0, tiled=True)
    out_piece = swap_half(out_weight, zh, 1)
    out_full = lax.all_gather(out_piece, "p", axis=0, tiled=True)
    flat_in = in_full.reshape(in_full.shape[0], 3 * half)
    projected = jnp.dot(gathered, flat_in, preferred_element_type=jnp.float32)
    projected = projected.astype(jnp.bfloat16).reshape(col_rows, 3, half)
    first_row = lax.axis_index("p") * col_rows
    own_points = first_row + jnp.arange(col_rows, dtype=jnp.int32)
    own_position = doc_position(own_points, doc_lengths)
    columns = lax.axis_size("p")
    ahead = [(i, i + 1) for i in range(columns - 1)]
    my_taps = lax.dynamic_slice_in_dim(short_taps, zh * half, half, 2)
    my_filter = lax.dynamic_slice_in_dim(filter_taps, zh * half, half, 1)
    my_decay = lax.dynamic_slice_in_dim(decay_rate, zh * half, half, 0)
    edge_rows = lax.ppermute(projected[col_rows - 2 :], "p", ahead)
    short_all = short_filter(
        jnp.concatenate([edge_rows, projected], 0), my_taps, own_position, col_rows
    )
    kv_product = (short_all[:, 1] * short_all[:, 2]).astype(jnp.bfloat16)
    tail_rows = lax.ppermute(kv_product[col_rows - tap_count :], "p", ahead)
    extended = jnp.concatenate([tail_rows, kv_product], 0)
    query = short_all[:, 0]
    shaped = my_filter * jnp.exp(
        -my_decay[None, :] * jnp.arange(tap_count, dtype=jnp.float32)[:, None]
    )
    long_mix = long_filter(extended, shaped, own_position, col_rows, tap_count)
    gated_mix = (query * long_mix).astype(jnp.bfloat16)
    summed = lax.psum_scatter(
        lax.dot_general(
            gated_mix, out_full, (((1,), (1,)), ((), ())), preferred_element_type=jnp.float32
        ).astype(jnp.bfloat16),
        COL,
        scatter_dimension=0,
        tiled=True,
    ).astype(jnp.float32)
    return (widened + summed).astype(jnp.bfloat16)


def solution(mesh):
    fsdp, tp = (mesh.shape["fsdp"], mesh.shape["tp"])
    grid = mesh.devices.reshape(fsdp // 2, 2, tp // 2, 2)
    fine = Mesh(grid, ("p", "zh", "zl", "c"))
    rows = ("p", "zh", "zl", "c")
    chan = ("zl", "c")
    in_specs = (
        P(rows, None),
        P(("p", "zh"), None, chan),
        P(("p", "zh"), chan),
        P(None, None, chan),
        P(None, chan),
        P(chan),
        P(),
    )
    out_specs = P(rows, None)
    return jax.shard_map(body, mesh=fine, in_specs=in_specs, out_specs=out_specs, check_vma=False)
```

profile of v0, /device:TPU:6, one launch (start us, length us, event | category | flops | bytes accessed | tf_op | source)
XLA Modules:
  0.0 328.6 jit_solution(9179054055207928626)
XLA Ops:
  6.5 1.1 fusion.25
  8.1 7.3 %collective-permute-start = (bf16[128,3,256]{0,2,1:T(8,128)(2,1)S(1)}, bf16[128,3,256]{0,2,1:T(8,128)(2,1)S(1)}, u32[]{:S(2)}, u32[]{:S(2)}) collective-permute-start(bf16[128,3,256]{0,2,1:T(8,128)(2,1)S(1)} %broadcast_select_fusion.2), channel_id=1, source_target_pairs={{0,8},{8,0},{1,9},{9,1},{2,10},{10,2},{3,11},{11,3},{4,12},{12,4},... | collective-permute-start | bytes 589832 | tf_op jit(solution)/shard_map/ppermute | solution.py:50
  15.3 5.0 %collective-permute-done = bf16[128,3,256]{0,2,1:T(8,128)(2,1)S(1)} collective-permute-done((bf16[128,3,256]{0,2,1:T(8,128)(2,1)S(1)}, bf16[128,3,256]{0,2,1:T(8,128)(2,1)S(1)}, u32[]{:S(2)}, u32[]{:S(2)}) %collective-permute-start) | collective-permute-done | bytes 196640 | tf_op jit(solution)/shard_map/ppermute | solution.py:50
  20.4 0.8 pad_maximum_fusion.2
  21.5 1.0 fusion.17
  22.5 9.2 %collective-permute-start.3 = (bf16[128,256]{1,0:T(8,128)(2,1)S(1)}, bf16[128,256]{1,0:T(8,128)(2,1)S(1)}, u32[]{:S(2)}, u32[]{:S(2)}) collective-permute-start(bf16[128,256]{1,0:T(8,128)(2,1)S(1)} %broadcast_select_fusion.6), channel_id=1, source_target_pairs={{0,8},{8,0},{1,9},{9,1},{2,10},{10,2},{3,11},{11,3},{4,12},{12,4},... | collective-permute-start | bytes 196616 | tf_op jit(solution)/shard_map/ppermute | solution.py:50
  32.4 1.9 collective-permute-done.3
  34.2 63.8 %all-gather.6.cloned.1.call-done = bf16[4096,3,256]{0,2,1:T(8,128)(2,1)} async-done(((bf16[256,3,256]{0,2,1:T(8,128)(2,1)}), bf16[4096,3,256]{0,2,1:T(8,128)(2,1)}) %all-gather.6.cloned.1.call-update) | async-done | bytes 6291472 | tf_op jit(solution)/shard_map/all_gather | solution.py:69
  98.0 57.4 %all-gather.4.cloned.1.call-done = bf16[1024,4096]{1,0:T(8,128)(2,1)} async-done(((bf16[64,4096]{1,0:T(8,128)(2,1)}), bf16[1024,4096]{1,0:T(8,128)(2,1)}) %all-gather.4.cloned.1.call-update) | async-done | bytes 8388624 | tf_op jit(solution)/shard_map/all_gather | solution.py:67
  155.4 11.0 %convolution_convert_fusion.1 = bf16[1024,768]{1,0:T(8,128)(2,1)S(1)} fusion(bf16[1024,4096]{1,0:T(8,128)(2,1)} %all-gather.4.cloned.1.call-done, bf16[4096,768]{0,1:T(8,128)(2,1)} %bitcast.91), kind=kOutput, calls=%fused_computation.52 | convolution fusion | flops 6443237376 | bytes 16252928 | tf_op jit(solution)/shard_map/dot_general | solution.py:73
  166.4 1.2 copy-done.3
  167.8 3.4 %collective-permute-start.1 = (bf16[2,3,256]{0,2,1:T(8,128)(2,1)S(1)}, bf16[2,3,256]{0,2,1:T(8,128)(2,1)S(1)}, u32[]{:S(2)}, u32[]{:S(2)}) collective-permute-start(bf16[2,3,256]{0,2,1:T(8,128)(2,1)S(1)} %bitcast.73), channel_id=1, source_target_pairs={{0,16},{16,32},{32,48},{48,64},{64,80},{80,96},{96,112},{112,128},... | collective-permute-start | bytes 9224 | tf_op jit(solution)/shard_map/ppermute | solution.py:83
  171.2 0.7 pad_maximum_fusion.3
  171.9 1.7 copy.22
  173.7 3.1 collective-permute-done.1
  176.8 2.3 select_add_fusion.1
  179.2 5.7 %collective-permute-start.2 = (bf16[128,256]{0,1:T(8,128)(2,1)S(1)}, bf16[128,256]{0,1:T(8,128)(2,1)S(1)}, u32[]{:S(2)}, u32[]{:S(2)}) collective-permute-start(bf16[128,256]{0,1:T(8,128)(2,1)S(1)} %slice_bitcast_fusion.1), channel_id=1, source_target_pairs={{0,16},{16,32},{32,48},{48,64},{64,80},{80,96},{96,112},{112,128},... | collective-permute-start | bytes 196616 | tf_op jit(solution)/shard_map/ppermute | solution.py:88
  185.0 1.6 collective-permute-done.2
  186.6 0.2 copy.24
  186.9 54.6 %while.17 = (s32[]{:T(128)}, f32[1024,256]{1,0:T(8,128)S(1)}, s32[1024]{0:T(1024)S(1)}, f32[128,256]{1,0:T(8,128)S(1)}, bf16[1152,256]{1,0:T(8,128)(2,1)S(1)}, /...) while((s32[]{:T(128)}, f32[1024,256]{1,0:T(8,128)S(1)}, ...), condition=%wide.region_4.5_spmd.clone, body=%wide.region_3.4_spmd.clone.sunk | while | flops 17055876 | bytes 10573783 | solution.py:41
  187.3 6.4 %fusion.31 = f32[1024,256]{1,0:T(8,128)S(1)} fusion(f32[1024,256]{1,0:T(8,128)S(1)} %get-tuple-element.431, bf16[1152,256]{1,0:T(8,128)(2,1)S(1)} %get-tuple-element.473, s32[]{:T(128)S(6)} %select_n.767, f32[256]{0:T(256)S(1)} %bitcast.75, s32[]{:T(128)S(6)} %select_n.784, f32[256]{0:T(256)S(1)} %bitcast.76, s32[]{:T(128)S(6)} %select_n.785, ...), kind=kLoop, calls=%fused_computation.15.clone.1 | loop fusion | flops 17039360 | bytes 10518593 | tf_op jit(solution)/shard_map/while/body/eval_jaxpr/add | solution.py:35
  194.1 6.4 %fusion.31 = f32[1024,256]{1,0:T(8,128)S(1)} fusion(f32[1024,256]{1,0:T(8,128)S(1)} %get-tuple-element.431, bf16[1152,256]{1,0:T(8,128)(2,1)S(1)} %get-tuple-element.473, s32[]{:T(128)S(6)} %select_n.767, f32[256]{0:T(256)S(1)} %bitcast.75, s32[]{:T(128)S(6)} %select_n.784, f32[256]{0:T(256)S(1)} %bitcast.76, s32[]{:T(128)S(6)} %select_n.785, ...), kind=kLoop, calls=%fused_computation.15.clone.1 | loop fusion | flops 17039360 | bytes 10518593 | tf_op jit(solution)/shard_map/while/body/eval_jaxpr/add | solution.py:35
  200.9 6.4 %fusion.31 = f32[1024,256]{1,0:T(8,128)S(1)} fusion(f32[1024,256]{1,0:T(8,128)S(1)} %get-tuple-element.431, bf16[1152,256]{1,0:T(8,128)(2,1)S(1)} %get-tuple-element.473, s32[]{:T(128)S(6)} %select_n.767, f32[256]{0:T(256)S(1)} %bitcast.75, s32[]{:T(128)S(6)} %select_n.784, f32[256]{0:T(256)S(1)} %bitcast.76, s32[]{:T(128)S(6)} %select_n.785, ...), kind=kLoop, calls=%fused_computation.15.clone.1 | loop fusion | flops 17039360 | bytes 10518593 | tf_op jit(solution)/shard_map/while/body/eval_jaxpr/add | solution.py:35
  207.8 6.4 %fusion.31 = f32[1024,256]{1,0:T(8,128)S(1)} fusion(f32[1024,256]{1,0:T(8,128)S(1)} %get-tuple-element.431, bf16[1152,256]{1,0:T(8,128)(2,1)S(1)} %get-tuple-element.473, s32[]{:T(128)S(6)} %select_n.767, f32[256]{0:T(256)S(1)} %bitcast.75, s32[]{:T(128)S(6)} %select_n.784, f32[256]{0:T(256)S(1)} %bitcast.76, s32[]{:T(128)S(6)} %select_n.785, ...), kind=kLoop, calls=%fused_computation.15.clone.1 | loop fusion | flops 17039360 | bytes 10518593 | tf_op jit(solution)/shard_map/while/body/eval_jaxpr/add | solution.py:35
  214.6 6.4 %fusion.31 = f32[1024,256]{1,0:T(8,128)S(1)} fusion(f32[1024,256]{1,0:T(8,128)S(1)} %get-tuple-element.431, bf16[1152,256]{1,0:T(8,128)(2,1)S(1)} %get-tuple-element.473, s32[]{:T(128)S(6)} %select_n.767, f32[256]{0:T(256)S(1)} %bitcast.75, s32[]{:T(128)S(6)} %select_n.784, f32[256]{0:T(256)S(1)} %bitcast.76, s32[]{:T(128)S(6)} %select_n.785, ...), kind=kLoop, calls=%fused_computation.15.clone.1 | loop fusion | flops 17039360 | bytes 10518593 | tf_op jit(solution)/shard_map/while/body/eval_jaxpr/add | solution.py:35
  221.4 6.4 %fusion.31 = f32[1024,256]{1,0:T(8,128)S(1)} fusion(f32[1024,256]{1,0:T(8,128)S(1)} %get-tuple-element.431, bf16[1152,256]{1,0:T(8,128)(2,1)S(1)} %get-tuple-element.473, s32[]{:T(128)S(6)} %select_n.767, f32[256]{0:T(256)S(1)} %bitcast.75, s32[]{:T(128)S(6)} %select_n.784, f32[256]{0:T(256)S(1)} %bitcast.76, s32[]{:T(128)S(6)} %select_n.785, ...), kind=kLoop, calls=%fused_computation.15.clone.1 | loop fusion | flops 17039360 | bytes 10518593 | tf_op jit(solution)/shard_map/while/body/eval_jaxpr/add | solution.py:35
  228.2 6.4 %fusion.31 = f32[1024,256]{1,0:T(8,128)S(1)} fusion(f32[1024,256]{1,0:T(8,128)S(1)} %get-tuple-element.431, bf16[1152,256]{1,0:T(8,128)(2,1)S(1)} %get-tuple-element.473, s32[]{:T(128)S(6)} %select_n.767, f32[256]{0:T(256)S(1)} %bitcast.75, s32[]{:T(128)S(6)} %select_n.784, f32[256]{0:T(256)S(1)} %bitcast.76, s32[]{:T(128)S(6)} %select_n.785, ...), kind=kLoop, calls=%fused_computation.15.clone.1 | loop fusion | flops 17039360 | bytes 10518593 | tf_op jit(solution)/shard_map/while/body/eval_jaxpr/add | solution.py:35
  235.1 6.4 %fusion.31 = f32[1024,256]{1,0:T(8,128)S(1)} fusion(f32[1024,256]{1,0:T(8,128)S(1)} %get-tuple-element.431, bf16[1152,256]{1,0:T(8,128)(2,1)S(1)} %get-tuple-element.473, s32[]{:T(128)S(6)} %select_n.767, f32[256]{0:T(256)S(1)} %bitcast.75, s32[]{:T(128)S(6)} %select_n.784, f32[256]{0:T(256)S(1)} %bitcast.76, s32[]{:T(128)S(6)} %select_n.785, ...), kind=kLoop, calls=%fused_computation.15.clone.1 | loop fusion | flops 17039360 | bytes 10518593 | tf_op jit(solution)/shard_map/while/body/eval_jaxpr/add | solution.py:35
  241.5 0.3 copy.25
  241.9 7.6 %convolution_convert_fusion = bf16[1024,4096]{1,0:T(8,128)(2,1)} fusion(bf16[4096,256]{1,0:T(8,128)(2,1)} %all-gather.8.cloned.1.call-done, f32[1024,256]{0,1:T(8,128)S(1)} %copy.25, f32[1024,3,256]{0,2,1:T(8,128)} %copy-done), kind=kOutput, calls=%fused_computation.48 | convolution fusion | flops 2152202240 | bytes 12582912 | tf_op jit(solution)/shard_map/dot_general | solution.py:97
  249.5 70.6 %reduce-scatter.2.cloned.1.call-done = bf16[64,4096]{1,0:T(8,128)(2,1)} async-done(((bf16[1024,4096]{1,0:T(8,128)(2,1)}), bf16[64,4096]{1,0:T(8,128)(2,1)}) %reduce-scatter.2.cloned.1.call-update) | async-done | bytes 524304 | tf_op jit(solution)/shard_map/reduce_scatter | solution.py:96
  320.1 2.0 fusion.18
  (68 shorter events, 3.0 us)
Async XLA Ops:
  6.5 14.7 %copy-start.1 = (bf16[64,4096]{1,0:T(8,128)(2,1)S(1)}, bf16[64,4096]{1,0:T(8,128)(2,1)}, u32[]{:S(2)}) copy-start(bf16[64,4096]{1,0:T(8,128)(2,1)} %param.9) | copy-start | bytes 1572868
  6.5 91.5 %all-gather.6.cloned.1.call-start = ((), (), s32[]{:S(2)}) async-start(), calls=%async_computation.2 | async-start | bytes 6684672 | tf_op jit(solution)/shard_map/all_gather | solution.py:69
  6.5 16.0 %copy-start.4 = (bf16[128,512]{1,0:T(8,128)(2,1)S(1)}, bf16[128,512]{1,0:T(8,128)(2,1)}, u32[]{:S(2)}) copy-start(bf16[128,512]{1,0:T(8,128)(2,1)} %param.11) | copy-start | bytes 393220
  6.5 25.2 %copy-start.7 = (s32[64]{0:T(128)S(1)}, s32[64]{0:T(128)}, u32[]{:S(2)}) copy-start(s32[64]{0:T(128)} %param.15) | copy-start | bytes 772
  7.7 24.4 %copy-start.8 = (f32[512]{0:T(512)S(1)}, f32[512]{0:T(512)}, u32[]{:S(2)}) copy-start(f32[512]{0:T(512)} %param.14) | copy-start | bytes 6148
  7.7 24.6 %copy-start.5 = (f32[128,512]{1,0:T(8,128)S(1)}, f32[128,512]{1,0:T(8,128)}, u32[]{:S(2)}) copy-start(f32[128,512]{1,0:T(8,128)} %param.13) | copy-start | bytes 786436
  7.7 24.6 %copy-start.6 = (f32[3,3,512]{2,1,0:T(4,128)S(1)}, f32[3,3,512]{2,1,0:T(4,128)}, u32[]{:S(2)}) copy-start(f32[3,3,512]{2,1,0:T(4,128)} %param.12) | copy-start | bytes 55300
  8.1 12.3 %collective-permute-start = (bf16[128,3,256]{0,2,1:T(8,128)(2,1)S(1)}, bf16[128,3,256]{0,2,1:T(8,128)(2,1)S(1)}, u32[]{:S(2)}, u32[]{:S(2)}) collective-permute-start(bf16[128,3,256]{0,2,1:T(8,128)(2,1)S(1)} %broadcast_select_fusion.2), channel_id=1, source_target_pairs={{0,8},{8,0},{1,9},{9,1},{2,10},{10,2},{3,11},{11,3},{4,12},{12,4},... | collective-permute-start | bytes 589832 | tf_op jit(solution)/shard_map/ppermute | solution.py:50
  21.2 134.2 %all-gather.4.cloned.1.call-start = ((), (), s32[]{:S(2)}) async-start(), calls=%async_computation.1 | async-start | bytes 8912896 | tf_op jit(solution)/shard_map/all_gather | solution.py:67
  22.5 219.4 %all-gather.8.cloned.1.call-start = ((), (), s32[]{:S(2)}) async-start(), calls=%async_computation.3 | async-start | bytes 2228224 | tf_op jit(solution)/shard_map/all_gather | solution.py:71
  22.5 11.7 %collective-permute-start.3 = (bf16[128,256]{1,0:T(8,128)(2,1)S(1)}, bf16[128,256]{1,0:T(8,128)(2,1)S(1)}, u32[]{:S(2)}, u32[]{:S(2)}) collective-permute-start(bf16[128,256]{1,0:T(8,128)(2,1)S(1)} %broadcast_select_fusion.6), channel_id=1, source_target_pairs={{0,8},{8,0},{1,9},{9,1},{2,10},{10,2},{3,11},{11,3},{4,12},{12,4},... | collective-permute-start | bytes 196616 | tf_op jit(solution)/shard_map/ppermute | solution.py:50
  166.4 1.2 copy-start.3
  167.8 8.9 %collective-permute-start.1 = (bf16[2,3,256]{0,2,1:T(8,128)(2,1)S(1)}, bf16[2,3,256]{0,2,1:T(8,128)(2,1)S(1)}, u32[]{:S(2)}, u32[]{:S(2)}) collective-permute-start(bf16[2,3,256]{0,2,1:T(8,128)(2,1)S(1)} %bitcast.73), channel_id=1, source_target_pairs={{0,16},{16,32},{32,48},{48,64},{64,80},{80,96},{96,112},{112,128},... | collective-permute-start | bytes 9224 | tf_op jit(solution)/shard_map/ppermute | solution.py:83
  171.9 148.2 %reduce-scatter.2.cloned.1.call-start = ((), (), s32[]{:S(2)}) async-start(), calls=%async_computation.4 | async-start | bytes 8912896 | tf_op jit(solution)/shard_map/reduce_scatter | solution.py:96
  179.0 7.6 %copy-start = (f32[1024,3,256]{0,2,1:T(8,128)}, f32[1024,3,256]{0,2,1:T(8,128)S(1)}, u32[]{:S(2)}) copy-start(f32[1024,3,256]{0,2,1:T(8,128)S(1)} %select_add_fusion.1) | copy-start | bytes 9437188
  179.2 7.4 %collective-permute-start.2 = (bf16[128,256]{0,1:T(8,128)(2,1)S(1)}, bf16[128,256]{0,1:T(8,128)(2,1)S(1)}, u32[]{:S(2)}, u32[]{:S(2)}) collective-permute-start(bf16[128,256]{0,1:T(8,128)(2,1)S(1)} %slice_bitcast_fusion.1), channel_id=1, source_target_pairs={{0,16},{16,32},{32,48},{48,64},{64,80},{80,96},{96,112},{112,128},... | collective-permute-start | bytes 196616 | tf_op jit(solution)/shard_map/ppermute | solution.py:88
  249.4 70.6 %copy-start.2 = (bf16[64,4096]{1,0:T(8,128)(2,1)S(1)}, bf16[64,4096]{1,0:T(8,128)(2,1)}, u32[]{:S(2)}) copy-start(bf16[64,4096]{1,0:T(8,128)(2,1)} %param.9) | copy-start | bytes 1572868
Sparse Core Ops, SparseCore 0:
  21.3 76.6 all-gather.5
  99.8 55.5 all-gather.3
  172.0 47.8 all-gather.7
  249.6 70.4 reduce-scatter.1
where the time goes:
time: 329 us
  waiting for transfers between devices  203 us (62%)
  other arithmetic  59.4 us (18%)
  starting transfers between devices  25.6 us (8%)
  matrix products  18.6 us (6%)
  between operations  13.4 us (4%)
  local copies, waits for them, and re-layouts  5.96 us (2%)
    reduce_scatter x1, waiting for transfers between devices, body(): lax.psum_scatter(lax.dot_general(gated_mix, out_full, (((1,), (1,)), ((),...  70.6 us
    all_gather x1, waiting for transfers between devices, body(): in_full = lax.all_gather(in_piece, 'p', axis=0, tiled=True)  63.8 us
    all_gather x1, waiting for transfers between devices, body(): gathered = lax.all_gather(normed, COL, axis=0, tiled=True)  57.4 us
    add x8, other arithmetic, tap_group(): running + jnp.where(inside, weight_row * window.astype(jnp.float32), jnp....  51.3 us
    ppermute x2, starting transfers between devices, swap_half(): got = lax.ppermute(give, 'zh', [(0, 1), (1, 0)])  16.4 us
    dot_general x1, matrix products, body(): projected = jnp.dot(gathered, flat_in, preferred_element_type=jnp.float32)  11 us
    dot_general x1, matrix products, body(): lax.dot_general(gated_mix, out_full, (((1,), (1,)), ((), ())), preferred_...  7.58 us
    ppermute x2, waiting for transfers between devices, swap_half(): got = lax.ppermute(give, 'zh', [(0, 1), (1, 0)])  6.86 us
  transfers between devices with their start and end apart: 8, of which 7 were waited for; matrix products, arithmetic and copies ran while one was open for 18% of the time, Pallas kernels for 0%

commit v1 on v0

--- a/solution.py
+++ b/solution.py
@@ -64,7 +64,9 @@
     normed = (
         widened * lax.rsqrt(jnp.mean(widened * widened, axis=1, keepdims=True) + 1e-06)
     ).astype(jnp.bfloat16)
-    gathered = lax.all_gather(normed, COL, axis=0, tiled=True)
+    gathered = jnp.concatenate(
+        lax.all_to_all(jnp.stack([normed] * lax.axis_size(COL)), COL, 0, 0), axis=0
+    )
     in_piece = swap_half(in_weight, zh, 2)
     in_full = lax.all_gather(in_piece, "p", axis=0, tiled=True)
     out_piece = swap_half(out_weight, zh, 1)

time: 329 us -> 461 us (1.40)
  waiting for transfers between devices: 203 us -> 332 us
    ppermute x2, waiting for transfers between devices: 6.86 us -> 195 us  [swap_half(): got = lax.ppermute(give, 'zh', [(0, 1), (1, 0)])]
    all_gather x1 -> x0, waiting for transfers between devices: 57.4 us -> none  [body(): gathered = lax.all_gather(normed, COL, axis=0, tiled=True)]
    ppermute x2, starting transfers between devices: 16.4 us -> 6.39 us  [swap_half(): got = lax.ppermute(give, 'zh', [(0, 1), (1, 0)])]
    all_to_all x0 -> x1, starting transfers between devices: none -> 8.75 us  [body(): lax.all_to_all(jnp.stack([normed] * lax.axis_size(COL)), COL, 0, 0)]
  transfers between devices with their start and end apart: 8 -> 8, of which waited for: 7 -> 6; matrix products, arithmetic and copies ran while one was open for 18% -> 13% of each run, Pallas kernels for 0% -> 0%
where the time goes in v1:
time: 461 us; the launch traced here: 460 us
  waiting for transfers between devices  332 us (72%)
  other arithmetic  60.7 us (13%)
  starting transfers between devices  24.3 us (5%)
  matrix products  18.6 us (4%)
  between operations  13.4 us (3%)
  local copies, waits for them, and re-layouts  9.21 us (2%)
    ppermute x2, waiting for transfers between devices, swap_half(): got = lax.ppermute(give, 'zh', [(0, 1), (1, 0)])  195 us
    reduce_scatter x1, waiting for transfers between devices, body(): lax.psum_scatter(lax.dot_general(gated_mix, out_full, (((1,), (1,)), ((),...  72.7 us
    all_gather x1, waiting for transfers between devices, body(): in_full = lax.all_gather(in_piece, 'p', axis=0, tiled=True)  61 us
    add x8, other arithmetic, tap_group(): running + jnp.where(inside, weight_row * window.astype(jnp.float32), jnp....  51.4 us
    dot_general x1, matrix products, body(): projected = jnp.dot(gathered, flat_in, preferred_element_type=jnp.float32)  11 us
  transfers between devices with their start and end apart: 8, of which 6 were waited for; matrix products, arithmetic and copies ran while one was open for 13% of the time, Pallas kernels for 0%

profile of v1, /device:TPU:6, one launch (start us, length us, event | category | flops | bytes accessed | tf_op | source)
XLA Modules:
  0.0 460.2 jit_solution(17635867757282137895)
XLA Ops:
  6.5 1.2 fusion.16
  7.8 1.2 fusion.17
  9.0 4.3 stack.2
  13.3 8.8 %all-to-all-start = ((bf16[16,64,4096]{2,1,0:T(8,128)(2,1)}), bf16[16,64,4096]{2,1,0:T(8,128)(2,1)}, u32[]{:S(2)}, u32[]{:S(2)}) async-start(bf16[16,64,4096]{2,1,0:T(8,128)(2,1)} %stack.2), calls=%async_computation | async-start | bytes 16777216 | tf_op jit(solution)/shard_map/all_to_all | solution.py:68
  22.6 5.9 %collective-permute-start = (bf16[128,3,256]{0,2,1:T(8,128)(2,1)S(1)}, bf16[128,3,256]{0,2,1:T(8,128)(2,1)S(1)}, u32[]{:S(2)}, u32[]{:S(2)}) collective-permute-start(bf16[128,3,256]{0,2,1:T(8,128)(2,1)S(1)} %broadcast_select_fusion.2), channel_id=1, source_target_pairs={{0,8},{8,0},{1,9},{9,1},{2,10},{10,2},{3,11},{11,3},{4,12},{12,4},... | collective-permute-start | bytes 589832 | tf_op jit(solution)/shard_map/ppermute | solution.py:50
  28.5 186.9 %collective-permute-done = bf16[128,3,256]{0,2,1:T(8,128)(2,1)S(1)} collective-permute-done((bf16[128,3,256]{0,2,1:T(8,128)(2,1)S(1)}, bf16[128,3,256]{0,2,1:T(8,128)(2,1)S(1)}, u32[]{:S(2)}, u32[]{:S(2)}) %collective-permute-start) | collective-permute-done | bytes 196640 | tf_op jit(solution)/shard_map/ppermute | solution.py:50
  215.4 0.8 pad_maximum_fusion.2
  216.3 0.5 collective-permute-start.3
  217.5 7.8 %collective-permute-done.3 = bf16[128,256]{1,0:T(8,128)(2,1)S(1)} collective-permute-done((bf16[128,256]{1,0:T(8,128)(2,1)S(1)}, bf16[128,256]{1,0:T(8,128)(2,1)S(1)}, u32[]{:S(2)}, u32[]{:S(2)}) %collective-permute-start.3) | collective-permute-done | bytes 65568 | tf_op jit(solution)/shard_map/ppermute | solution.py:50
  225.3 61.0 %all-gather.3.cloned.1.call-done = bf16[4096,3,256]{0,2,1:T(8,128)(2,1)} async-done(((bf16[256,3,256]{0,2,1:T(8,128)(2,1)}), bf16[4096,3,256]{0,2,1:T(8,128)(2,1)}) %all-gather.3.cloned.1.call-update) | async-done | bytes 6291472 | tf_op jit(solution)/shard_map/all_gather | solution.py:71
  286.4 11.0 %convolution_convert_fusion.1 = bf16[1024,768]{1,0:T(8,128)(2,1)S(1)} fusion(bf16[1024,4096]{1,0:T(8,128)(2,1)} %bitcast.2, bf16[4096,768]{0,1:T(8,128)(2,1)} %bitcast.92), kind=kOutput, calls=%fused_computation.52 | convolution fusion | flops 6443237376 | bytes 16252928 | tf_op jit(solution)/shard_map/dot_general | solution.py:75
  297.4 1.2 copy-done.2
  298.7 3.4 collective-permute-start.1
  302.1 0.7 pad_maximum_fusion.3
  302.8 1.7 copy.22
  304.6 1.7 collective-permute-done.1
  306.3 2.3 select_add_fusion.1
  308.8 5.6 %collective-permute-start.2 = (bf16[128,256]{0,1:T(8,128)(2,1)S(1)}, bf16[128,256]{0,1:T(8,128)(2,1)S(1)}, u32[]{:S(2)}, u32[]{:S(2)}) collective-permute-start(bf16[128,256]{0,1:T(8,128)(2,1)S(1)} %slice_bitcast_fusion.1), channel_id=1, source_target_pairs={{0,16},{16,32},{32,48},{48,64},{64,80},{80,96},{96,112},{112,128},... | collective-permute-start | bytes 196616 | tf_op jit(solution)/shard_map/ppermute | solution.py:90
  314.5 1.6 collective-permute-done.2
  316.4 54.6 %while.17 = (s32[]{:T(128)}, f32[1024,256]{1,0:T(8,128)S(1)}, s32[1024]{0:T(1024)S(1)}, f32[128,256]{1,0:T(8,128)S(1)}, bf16[1152,256]{1,0:T(8,128)(2,1)S(1)}, /...) while((s32[]{:T(128)}, f32[1024,256]{1,0:T(8,128)S(1)}, ...), condition=%wide.region_4.5_spmd.clone, body=%wide.region_3.4_spmd.clone.sunk | while | flops 17055876 | bytes 10573791 | solution.py:41
  316.8 6.4 %fusion.31 = f32[1024,256]{1,0:T(8,128)S(1)} fusion(f32[1024,256]{1,0:T(8,128)S(1)} %get-tuple-element.431, bf16[1152,256]{1,0:T(8,128)(2,1)S(1)} %get-tuple-element.473, s32[]{:T(128)S(6)} %select_n.767, f32[256]{0:T(256)S(1)} %bitcast.76, s32[]{:T(128)S(6)} %select_n.784, f32[256]{0:T(256)S(1)} %bitcast.77, s32[]{:T(128)S(6)} %select_n.785, ...), kind=kLoop, calls=%fused_computation.15.clone.1 | loop fusion | flops 17039360 | bytes 10518593 | tf_op jit(solution)/shard_map/while/body/eval_jaxpr/add | solution.py:35
  323.7 6.4 %fusion.31 = f32[1024,256]{1,0:T(8,128)S(1)} fusion(f32[1024,256]{1,0:T(8,128)S(1)} %get-tuple-element.431, bf16[1152,256]{1,0:T(8,128)(2,1)S(1)} %get-tuple-element.473, s32[]{:T(128)S(6)} %select_n.767, f32[256]{0:T(256)S(1)} %bitcast.76, s32[]{:T(128)S(6)} %select_n.784, f32[256]{0:T(256)S(1)} %bitcast.77, s32[]{:T(128)S(6)} %select_n.785, ...), kind=kLoop, calls=%fused_computation.15.clone.1 | loop fusion | flops 17039360 | bytes 10518593 | tf_op jit(solution)/shard_map/while/body/eval_jaxpr/add | solution.py:35
  330.5 6.4 %fusion.31 = f32[1024,256]{1,0:T(8,128)S(1)} fusion(f32[1024,256]{1,0:T(8,128)S(1)} %get-tuple-element.431, bf16[1152,256]{1,0:T(8,128)(2,1)S(1)} %get-tuple-element.473, s32[]{:T(128)S(6)} %select_n.767, f32[256]{0:T(256)S(1)} %bitcast.76, s32[]{:T(128)S(6)} %select_n.784, f32[256]{0:T(256)S(1)} %bitcast.77, s32[]{:T(128)S(6)} %select_n.785, ...), kind=kLoop, calls=%fused_computation.15.clone.1 | loop fusion | flops 17039360 | bytes 10518593 | tf_op jit(solution)/shard_map/while/body/eval_jaxpr/add | solution.py:35
  337.3 6.4 %fusion.31 = f32[1024,256]{1,0:T(8,128)S(1)} fusion(f32[1024,256]{1,0:T(8,128)S(1)} %get-tuple-element.431, bf16[1152,256]{1,0:T(8,128)(2,1)S(1)} %get-tuple-element.473, s32[]{:T(128)S(6)} %select_n.767, f32[256]{0:T(256)S(1)} %bitcast.76, s32[]{:T(128)S(6)} %select_n.784, f32[256]{0:T(256)S(1)} %bitcast.77, s32[]{:T(128)S(6)} %select_n.785, ...), kind=kLoop, calls=%fused_computation.15.clone.1 | loop fusion | flops 17039360 | bytes 10518593 | tf_op jit(solution)/shard_map/while/body/eval_jaxpr/add | solution.py:35
  344.1 6.4 %fusion.31 = f32[1024,256]{1,0:T(8,128)S(1)} fusion(f32[1024,256]{1,0:T(8,128)S(1)} %get-tuple-element.431, bf16[1152,256]{1,0:T(8,128)(2,1)S(1)} %get-tuple-element.473, s32[]{:T(128)S(6)} %select_n.767, f32[256]{0:T(256)S(1)} %bitcast.76, s32[]{:T(128)S(6)} %select_n.784, f32[256]{0:T(256)S(1)} %bitcast.77, s32[]{:T(128)S(6)} %select_n.785, ...), kind=kLoop, calls=%fused_computation.15.clone.1 | loop fusion | flops 17039360 | bytes 10518593 | tf_op jit(solution)/shard_map/while/body/eval_jaxpr/add | solution.py:35
  351.0 6.4 %fusion.31 = f32[1024,256]{1,0:T(8,128)S(1)} fusion(f32[1024,256]{1,0:T(8,128)S(1)} %get-tuple-element.431, bf16[1152,256]{1,0:T(8,128)(2,1)S(1)} %get-tuple-element.473, s32[]{:T(128)S(6)} %select_n.767, f32[256]{0:T(256)S(1)} %bitcast.76, s32[]{:T(128)S(6)} %select_n.784, f32[256]{0:T(256)S(1)} %bitcast.77, s32[]{:T(128)S(6)} %select_n.785, ...), kind=kLoop, calls=%fused_computation.15.clone.1 | loop fusion | flops 17039360 | bytes 10518593 | tf_op jit(solution)/shard_map/while/body/eval_jaxpr/add | solution.py:35
  357.8 6.4 %fusion.31 = f32[1024,256]{1,0:T(8,128)S(1)} fusion(f32[1024,256]{1,0:T(8,128)S(1)} %get-tuple-element.431, bf16[1152,256]{1,0:T(8,128)(2,1)S(1)} %get-tuple-element.473, s32[]{:T(128)S(6)} %select_n.767, f32[256]{0:T(256)S(1)} %bitcast.76, s32[]{:T(128)S(6)} %select_n.784, f32[256]{0:T(256)S(1)} %bitcast.77, s32[]{:T(128)S(6)} %select_n.785, ...), kind=kLoop, calls=%fused_computation.15.clone.1 | loop fusion | flops 17039360 | bytes 10518593 | tf_op jit(solution)/shard_map/while/body/eval_jaxpr/add | solution.py:35
  364.6 6.4 %fusion.31 = f32[1024,256]{1,0:T(8,128)S(1)} fusion(f32[1024,256]{1,0:T(8,128)S(1)} %get-tuple-element.431, bf16[1152,256]{1,0:T(8,128)(2,1)S(1)} %get-tuple-element.473, s32[]{:T(128)S(6)} %select_n.767, f32[256]{0:T(256)S(1)} %bitcast.76, s32[]{:T(128)S(6)} %select_n.784, f32[256]{0:T(256)S(1)} %bitcast.77, s32[]{:T(128)S(6)} %select_n.785, ...), kind=kLoop, calls=%fused_computation.15.clone.1 | loop fusion | flops 17039360 | bytes 10518593 | tf_op jit(solution)/shard_map/while/body/eval_jaxpr/add | solution.py:35
  371.1 0.3 copy.25
  371.4 7.6 %convolution_convert_fusion = bf16[1024,4096]{1,0:T(8,128)(2,1)} fusion(bf16[4096,256]{1,0:T(8,128)(2,1)} %all-gather.5.cloned.1.call-done, f32[1024,256]{0,1:T(8,128)S(1)} %copy.25, f32[1024,3,256]{0,2,1:T(8,128)} %copy-done), kind=kOutput, calls=%fused_computation.48 | convolution fusion | flops 2152202240 | bytes 12582912 | tf_op jit(solution)/shard_map/dot_general | solution.py:99
  379.0 72.7 %reduce-scatter.2.cloned.1.call-done = bf16[64,4096]{1,0:T(8,128)(2,1)} async-done(((bf16[1024,4096]{1,0:T(8,128)(2,1)}), bf16[64,4096]{1,0:T(8,128)(2,1)}) %reduce-scatter.2.cloned.1.call-update) | async-done | bytes 524304 | tf_op jit(solution)/shard_map/reduce_scatter | solution.py:98
  451.7 2.0 fusion.18
  (68 shorter events, 3.1 us)
Async XLA Ops:
  13.3 8.9 %copy-start.4 = (bf16[128,3,512]{2,0,1:T(8,128)(2,1)S(1)}, bf16[128,3,512]{2,0,1:T(8,128)(2,1)}, u32[]{:S(2)}) copy-start(bf16[128,3,512]{2,0,1:T(8,128)(2,1)} %param.10) | copy-start | bytes 1179652
  13.3 273.0 %all-to-all-start = ((bf16[16,64,4096]{2,1,0:T(8,128)(2,1)}), bf16[16,64,4096]{2,1,0:T(8,128)(2,1)}, u32[]{:S(2)}, u32[]{:S(2)}) async-start(bf16[16,64,4096]{2,1,0:T(8,128)(2,1)} %stack.2), calls=%async_computation | async-start | bytes 16777216 | tf_op jit(solution)/shard_map/all_to_all | solution.py:68
  22.1 194.2 %copy-start.3 = (bf16[128,512]{1,0:T(8,128)(2,1)S(1)}, bf16[128,512]{1,0:T(8,128)(2,1)}, u32[]{:S(2)}) copy-start(bf16[128,512]{1,0:T(8,128)(2,1)} %param.11) | copy-start | bytes 393220
  22.1 194.8 %copy-start.7 = (s32[64]{0:T(128)S(1)}, s32[64]{0:T(128)}, u32[]{:S(2)}) copy-start(s32[64]{0:T(128)} %param.15) | copy-start | bytes 772
  22.1 195.1 %copy-start.8 = (f32[512]{0:T(512)S(1)}, f32[512]{0:T(512)}, u32[]{:S(2)}) copy-start(f32[512]{0:T(512)} %param.14) | copy-start | bytes 6148
  22.1 195.3 %copy-start.5 = (f32[128,512]{1,0:T(8,128)S(1)}, f32[128,512]{1,0:T(8,128)}, u32[]{:S(2)}) copy-start(f32[128,512]{1,0:T(8,128)} %param.13) | copy-start | bytes 786436
  22.1 195.4 %copy-start.6 = (f32[3,3,512]{2,1,0:T(4,128)S(1)}, f32[3,3,512]{2,1,0:T(4,128)}, u32[]{:S(2)}) copy-start(f32[3,3,512]{2,1,0:T(4,128)} %param.12) | copy-start | bytes 55300
  22.1 264.2 %all-gather.3.cloned.1.call-start = ((), (), s32[]{:S(2)}) async-start(), calls=%async_computation.2 | async-start | bytes 6684672 | tf_op jit(solution)/shard_map/all_gather | solution.py:71
  22.6 192.8 %collective-permute-start = (bf16[128,3,256]{0,2,1:T(8,128)(2,1)S(1)}, bf16[128,3,256]{0,2,1:T(8,128)(2,1)S(1)}, u32[]{:S(2)}, u32[]{:S(2)}) collective-permute-start(bf16[128,3,256]{0,2,1:T(8,128)(2,1)S(1)} %broadcast_select_fusion.2), channel_id=1, source_target_pairs={{0,8},{8,0},{1,9},{9,1},{2,10},{10,2},{3,11},{11,3},{4,12},{12,4},... | collective-permute-start | bytes 589832 | tf_op jit(solution)/shard_map/ppermute | solution.py:50
  216.3 155.2 %all-gather.5.cloned.1.call-start = ((), (), s32[]{:S(2)}) async-start(), calls=%async_computation.3 | async-start | bytes 2228224 | tf_op jit(solution)/shard_map/all_gather | solution.py:73
  216.3 9.0 %collective-permute-start.3 = (bf16[128,256]{1,0:T(8,128)(2,1)S(1)}, bf16[128,256]{1,0:T(8,128)(2,1)S(1)}, u32[]{:S(2)}, u32[]{:S(2)}) collective-permute-start(bf16[128,256]{1,0:T(8,128)(2,1)S(1)} %broadcast_select_fusion.6), channel_id=1, source_target_pairs={{0,8},{8,0},{1,9},{9,1},{2,10},{10,2},{3,11},{11,3},{4,12},{12,4},... | collective-permute-start | bytes 196616 | tf_op jit(solution)/shard_map/ppermute | solution.py:50
  297.4 1.2 copy-start.2
  298.7 7.6 %collective-permute-start.1 = (bf16[2,3,256]{0,2,1:T(8,128)(2,1)S(1)}, bf16[2,3,256]{0,2,1:T(8,128)(2,1)S(1)}, u32[]{:S(2)}, u32[]{:S(2)}) collective-permute-start(bf16[2,3,256]{0,2,1:T(8,128)(2,1)S(1)} %bitcast.74), channel_id=1, source_target_pairs={{0,16},{16,32},{32,48},{48,64},{64,80},{80,96},{96,112},{112,128},... | collective-permute-start | bytes 9224 | tf_op jit(solution)/shard_map/ppermute | solution.py:85
  302.8 148.9 %reduce-scatter.2.cloned.1.call-start = ((), (), s32[]{:S(2)}) async-start(), calls=%async_computation.4 | async-start | bytes 8912896 | tf_op jit(solution)/shard_map/reduce_scatter | solution.py:98
  308.6 7.5 %copy-start = (f32[1024,3,256]{0,2,1:T(8,128)}, f32[1024,3,256]{0,2,1:T(8,128)S(1)}, u32[]{:S(2)}) copy-start(f32[1024,3,256]{0,2,1:T(8,128)S(1)} %select_add_fusion.1) | copy-start | bytes 9437188
  308.8 7.4 %collective-permute-start.2 = (bf16[128,256]{0,1:T(8,128)(2,1)S(1)}, bf16[128,256]{0,1:T(8,128)(2,1)S(1)}, u32[]{:S(2)}, u32[]{:S(2)}) collective-permute-start(bf16[128,256]{0,1:T(8,128)(2,1)S(1)} %slice_bitcast_fusion.1), channel_id=1, source_target_pairs={{0,16},{16,32},{32,48},{48,64},{64,80},{80,96},{96,112},{112,128},... | collective-permute-start | bytes 196616 | tf_op jit(solution)/shard_map/ppermute | solution.py:90
  379.0 72.7 %copy-start.1 = (bf16[64,4096]{1,0:T(8,128)(2,1)S(1)}, bf16[64,4096]{1,0:T(8,128)(2,1)}, u32[]{:S(2)}) copy-start(bf16[64,4096]{1,0:T(8,128)(2,1)} %param.9) | copy-start | bytes 1572868
Sparse Core Ops, SparseCore 0:
  216.4 69.9 all-gather.2
  302.9 50.3 all-gather.4
  379.2 72.5 reduce-scatter.1
